TPU v7x, 128 devices: a whole 4x4x4 slice. The times are simulated.
128 devices in a mesh: expert: 4 (over z_lo, core), fsdp: 32 (over y, z_hi, x).
Axes of the slice: x: 4, y: 4, z: 4 (z_hi: 2, z_lo: 2; z = z_hi * 2 + z_lo), core: 2. Of those that a mesh axis runs over, the one named last changes fastest.
Arguments:
- tokens: bfloat16 [16384, 2048], P(('expert', 'fsdp')), may hold values from -6 to 6
- expert_ids: int32 [16384, 1], P(('expert', 'fsdp')), may hold values from 0 to 7; in each aligned block of 128 rows (0 to 127, 128 to 255, ...) at most 24 rows name the same one
- gate_weight: bfloat16 [8, 2048, 8192], P('expert', None, 'fsdp'), may hold values from -0.125 to 0.125
- up_weight: bfloat16 [8, 2048, 8192], P('expert', None, 'fsdp'), may hold values from -0.125 to 0.125
- hidden_grad: bfloat16 [8, 3072, 8192], P('expert', None, 'fsdp'), may hold values from -0.1796875 to 0.1796875
Outputs:
- hidden: bfloat16 [8, 3072, 8192], P('expert', None, 'fsdp')
- gate_grad: float32 [8, 2048, 8192], P('expert', None, 'fsdp')
- up_grad: float32 [8, 2048, 8192], P('expert', None, 'fsdp')
Inputs may be any that keep to these rules, and one draw needn't show every extreme that they name: `expert_ids`: within the tokens of one device (aligned blocks of 128 rows) no expert is named more than 24 times, a bound that some block reaches.
All inputs are finite; a program needn't handle non-finite values.
Results may differ from a plain program's by a relative error of at most 0.003.
Values may be sent and summed in bfloat16 or wider, within the bound.
No kernel may reach another device: no remote copies, remote signals or barrier semaphores. Data moves between devices by JAX's collectives and lax.ppermute only.
A program may use at most 192 MiB of HBM per device.

v0:
```python
import jax
import jax.numpy as jnp
from jax import lax
from jax.sharding import PartitionSpec as P

CAP = 24


def make_fold(gate_part, up_part, grad_part, piece):
    groups, sources, count, model = piece.shape
    rows_flat = piece.reshape(groups, sources * count, model)
    gate = jnp.einsum("grd,gdf->grf", rows_flat, gate_part, preferred_element_type=jnp.float32)
    upval = jnp.einsum("grd,gdf->grf", rows_flat, up_part, preferred_element_type=jnp.float32)
    cotan = grad_part
    cotan = cotan.reshape(groups, sources * count, cotan.shape[3]).astype(jnp.float32)
    sigma = 1.0 / (1.0 + jnp.exp(-gate))
    active = gate * sigma
    hidden = (active * upval).astype(jnp.bfloat16)
    gate_delta = (cotan * upval * sigma * (1.0 + gate * (1.0 - sigma))).astype(jnp.bfloat16)
    up_delta = (cotan * active).astype(jnp.bfloat16)
    hidden_buf = hidden.reshape(groups, sources, count, hidden.shape[2])
    gate_sum = jnp.einsum("grd,grf->gdf", rows_flat, gate_delta, preferred_element_type=jnp.float32)
    up_sum = jnp.einsum("grd,grf->gdf", rows_flat, up_delta, preferred_element_type=jnp.float32)
    return (hidden_buf, gate_sum, up_sum)


def on_device(tokens, expert_ids, gate_weight, up_weight, hidden_grad):
    owners = lax.axis_size("expert")
    members = lax.axis_size("fsdp")
    per_owner = gate_weight.shape[0]
    model = gate_weight.shape[1]
    width = gate_weight.shape[2]
    route = expert_ids[:, 0]
    total_experts = per_owner * owners
    onehot = (route[:, None] == jnp.arange(total_experts, dtype=jnp.int32)[None, :]).astype(
        jnp.int32
    )
    rank = jnp.sum((jnp.cumsum(onehot, axis=0) - onehot) * onehot, axis=1)
    owner_of = route // per_owner
    within = route % per_owner
    target = within * (owners * CAP) + owner_of * CAP + rank
    send_rows = per_owner * owners * CAP
    placing = (jnp.arange(send_rows, dtype=jnp.int32)[:, None] == target[None, :]).astype(
        jnp.bfloat16
    )
    outgoing = jnp.dot(placing, tokens, preferred_element_type=jnp.float32).astype(jnp.bfloat16)
    outgoing = outgoing.reshape(per_owner, owners, CAP, model)
    slot_count = members * CAP
    grad_four = hidden_grad.reshape(per_owner, owners, slot_count, width)
    arrived = lax.all_to_all(outgoing, "expert", split_axis=1, concat_axis=1, tiled=True)
    hidden_buf, gate_sum, up_sum = make_fold(
        gate_weight, up_weight, grad_four, lax.all_gather(arrived, "fsdp", axis=2, tiled=True)
    )
    hidden = hidden_buf.reshape(per_owner, owners * slot_count, width)
    return (hidden, gate_sum, up_sum)


def solution(mesh):
    in_specs = (
        P(("expert", "fsdp"), None),
        P(("expert", "fsdp"), None),
        P("expert", None, "fsdp"),
        P("expert", None, "fsdp"),
        P("expert", None, "fsdp"),
    )
    out_specs = (P("expert", None, "fsdp"), P("expert", None, "fsdp"), P("expert", None, "fsdp"))
    return jax.shard_map(
        on_device, mesh=mesh, in_specs=in_specs, out_specs=out_specs, check_vma=False
    )
```

profile of v0, /device:TPU:1, one launch (start us, length us, event | category | flops | bytes accessed | tf_op | source)
XLA Modules:
  0.0 333.2 jit_solution(6977620930434274134)
XLA Ops:
  7.2 0.0 copy-start
  7.2 0.0 all-gather.2.cloned.1.call-start
  7.2 0.9 fusion.11
  8.1 0.2 reduce_window_sum.11
  8.3 0.8 select_reduce_fusion
  9.1 0.7 fusion.15
  9.8 1.4 convolution_convert_fusion
  11.2 0.1 copy.10
  11.3 15.2 %all_to_all.5 = bf16[2,4,24,2048]{3,2,0,1:T(8,128)(2,1)} all-to-all(bf16[2,4,24,2048]{3,2,0,1:T(8,128)(2,1)S(1)} %copy.10), channel_id=1, replica_groups=mesh['expert'=4,'fsdp'=32] {'expert'}, dimensions={1} | all-to-all | bytes 1572864 | tf_op jit(solution)/shard_map/all_to_all | solution.py:50
  26.5 0.0 all-gather.2.cloned.1.call-update
  26.5 211.1 %all-gather.2.cloned.1.call-done = bf16[2,4,768,2048]{3,2,0,1:T(8,128)(2,1)} async-done(((bf16[2,4,24,2048]{3,2,0,1:T(8,128)(2,1)}), bf16[2,4,768,2048]{3,2,0,1:T(8,128)(2,1)}) %all-gather.2.cloned.1.call-update) | async-done | bytes 25165840 | tf_op jit(solution)/shard_map/all_gather | solution.py:52
  237.6 0.0 copy-start.3
  237.6 21.2 %copy.11 = bf16[2,4,768,2048]{3,2,1,0:T(8,128)(2,1)} copy(bf16[2,4,768,2048]{3,2,0,1:T(8,128)(2,1)} %all-gather.2.cloned.1.call-done) | data formatting | bytes 50331648 | tf_op jit(solution)/shard_map/all_gather | solution.py:52
  258.8 0.0 copy-done.3
  258.8 0.0 copy-start.2
  258.8 14.5 %fusion.18 = f32[2,3072,256]{2,1,0:T(8,128)} fusion(bf16[2,3072,2048]{2,1,0:T(8,128)(2,1)} %bitcast.11, bf16[2,2048,256]{2,1,0:T(8,128)(2,1)S(1)} %copy-done.3), kind=kOutput, calls=%fused_computation.28 | convolution fusion | flops 6442450944 | bytes 33554432 | tf_op jit(solution)/shard_map/grd,gdf->grf/dot_general | solution.py:12
  273.3 0.0 copy-done.2
  273.3 17.5 %fusion.5 = f32[2,2048,256]{2,1,0:T(8,128)} fusion(bf16[2,3072,2048]{2,1,0:T(8,128)(2,1)} %bitcast.12, bf16[2,3072,256]{2,1,0:T(8,128)(2,1)S(1)} %copy-done.2, f32[2,3072,256]{2,1,0:T(8,128)} %fusion.18), kind=kOutput, calls=%fused_computation.9 | convolution fusion | flops 6453460992 | bytes 38797312 | tf_op jit(solution)/shard_map/grd,grf->gdf/dot_general | solution.py:23
  290.8 0.0 copy-done
  290.8 16.1 %multiply_convert_fusion = (bf16[2,3072,256]{2,1,0:T(8,128)(2,1)}, f32[2,3072,256]{2,1,0:T(8,128)}) fusion(f32[2,3072,256]{2,1,0:T(8,128)} %fusion.18, bf16[2,3072,2048]{2,1,0:T(8,128)(2,1)} %bitcast.13, bf16[2,2048,256]{2,1,0:T(8,128)(2,1)S(1)} %copy-done), kind=kOutput, calls=%fused_computation.6 | convolution fusion | flops 6451888128 | bytes 42991616 | tf_op jit(solution)/shard_map/grd,gdf->grf/dot_general | solution.py:13
  306.8 0.0 copy-start.1
  306.8 19.5 %fusion.7 = f32[2,2048,256]{2,1,0:T(8,128)} fusion(bf16[2,3072,2048]{2,1,0:T(8,128)(2,1)} %bitcast.14, f32[2,3072,256]{2,1,0:T(8,128)} %get-tuple-element.4, bf16[2,3072,256]{2,1,0:T(8,128)(2,1)S(1)} %copy-done.2, f32[2,3072,256]{2,1,0:T(8,128)} %fusion.18), kind=kOutput, calls=%fused_computation.10 | convolution fusion | flops 6459752448 | bytes 45088768 | tf_op jit(solution)/shard_map/grd,grf->gdf/dot_general | solution.py:22
  326.4 0.0 copy-done.1
Async XLA Ops:
  7.2 283.6 %copy-start = (bf16[2,2048,256]{2,1,0:T(8,128)(2,1)S(1)}, bf16[2,2048,256]{2,1,0:T(8,128)(2,1)}, u32[]{:S(2)}) copy-start(bf16[2,2048,256]{2,1,0:T(8,128)(2,1)} %param.8) | copy-start | bytes 6291460
  7.2 230.5 %all-gather.2.cloned.1.call-start = ((), (), s32[]{:S(2)}) async-start(), calls=%async_computation.1 | async-start | bytes 25952256 | tf_op jit(solution)/shard_map/all_gather | solution.py:52
  237.6 21.2 %copy-start.3 = (bf16[2,2048,256]{2,1,0:T(8,128)(2,1)S(1)}, bf16[2,2048,256]{2,1,0:T(8,128)(2,1)}, u32[]{:S(2)}) copy-start(bf16[2,2048,256]{2,1,0:T(8,128)(2,1)} %param.7) | copy-start | bytes 6291460
  258.8 14.5 %copy-start.2 = (bf16[2,3072,256]{2,1,0:T(8,128)(2,1)S(1)}, bf16[2,3072,256]{2,1,0:T(8,128)(2,1)}, u32[]{:S(2)}) copy-start(bf16[2,3072,256]{2,1,0:T(8,128)(2,1)} %param.9) | copy-start | bytes 9437188
  306.8 19.5 %copy-start.1 = (bf16[2,2048,256]{2,1,0:T(8,128)(2,1)S(1)}, bf16[2,2048,256]{2,1,0:T(8,128)(2,1)}, u32[]{:S(2)}) copy-start(bf16[2,2048,256]{2,1,0:T(8,128)(2,1)} %param.8) | copy-start | bytes 6291460
Sparse Core Ops, SparseCore 0:
  26.6 210.9 all-gather.1
where the time goes:
time: 334 us; the launch traced here: 333 us
  waiting for transfers between devices  211 us (63%)
  matrix products  68.9 us (21%)
  local copies, waits for them, and re-layouts  21.3 us (6%)
  blocking collectives  15.2 us (5%)
  between operations  14.1 us (4%)
    all_gather x1, waiting for transfers between devices, on_device(): lax.all_gather(arrived, 'fsdp', axis=2, tiled=True)  211 us
    all_gather x1, local copies, waits for them, and re-layouts, on_device(): lax.all_gather(arrived, 'fsdp', axis=2, tiled=True)  21.2 us
    dot_general x1, matrix products, make_fold(): jnp.einsum('grd,grf->gdf', rows_flat, gate_delta, preferred_element_type=...  19.5 us
    dot_general x1, matrix products, make_fold(): jnp.einsum('grd,grf->gdf', rows_flat, up_delta, preferred_element_type=jn...  17.5 us
    dot_general x1, matrix products, make_fold(): jnp.einsum('grd,gdf->grf', rows_flat, up_part, preferred_element_type=jnp...  16.1 us
    all_to_all x1, blocking collectives, on_device(): lax.all_to_all(outgoing, 'expert', split_axis=1, concat_axis=1, tiled=True)  15.2 us
    dot_general x1, matrix products, make_fold(): jnp.einsum('grd,gdf->grf', rows_flat, gate_part, preferred_element_type=j...  14.5 us
  transfers between devices with their start and end apart: 1, of which 1 were waited for; matrix products, arithmetic and copies ran while one was open for 0% of the time, Pallas kernels for 0%

commit v1 on v0

--- a/solution.py
+++ b/solution.py
@@ -49,7 +49,12 @@
     grad_four = hidden_grad.reshape(per_owner, owners, slot_count, width)
     arrived = lax.all_to_all(outgoing, "expert", split_axis=1, concat_axis=1, tiled=True)
     hidden_buf, gate_sum, up_sum = make_fold(
-        gate_weight, up_weight, grad_four, lax.all_gather(arrived, "fsdp", axis=2, tiled=True)
+        gate_weight,
+        up_weight,
+        grad_four,
+        jnp.concatenate(
+            lax.all_to_all(jnp.stack([arrived] * lax.axis_size("fsdp")), "fsdp", 0, 0), axis=2
+        ),
     )
     hidden = hidden_buf.reshape(per_owner, owners * slot_count, width)
     return (hidden, gate_sum, up_sum)

time: 334 us -> 408 us (1.22)
  the two profiles are of different devices: /device:TPU:1 before, /device:TPU:34 now
where the time goes in v1:
time: 408 us; the launch traced here: 407 us
  blocking collectives  311 us (76%)
  matrix products  68.7 us (17%)
  local copies, waits for them, and re-layouts  24.5 us (6%)
    all_to_all x1, blocking collectives, on_device(): lax.all_to_all(jnp.stack([arrived] * lax.axis_size('fsdp')), 'fsdp', 0, 0)  298 us
    reshape x1, local copies, waits for them, and re-layouts, on_device(): jnp.concatenate(lax.all_to_all(jnp.stack([arrived] * lax.axis_size('fsdp'...  21.2 us
    dot_general x1, matrix products, make_fold(): jnp.einsum('grd,grf->gdf', rows_flat, gate_delta, preferred_element_type=...  19.2 us
    dot_general x1, matrix products, make_fold(): jnp.einsum('grd,grf->gdf', rows_flat, up_delta, preferred_element_type=jn...  17.5 us
    dot_general x1, matrix products, make_fold(): jnp.einsum('grd,gdf->grf', rows_flat, up_part, preferred_element_type=jnp...  16.1 us
    dot_general x1, matrix products, make_fold(): jnp.einsum('grd,gdf->grf', rows_flat, gate_part, preferred_element_type=j...  14.5 us
    all_to_all x1, blocking collectives, on_device(): lax.all_to_all(outgoing, 'expert', split_axis=1, concat_axis=1, tiled=True)  13.1 us

profile of v1, /device:TPU:34, one launch (start us, length us, event | category | flops | bytes accessed | tf_op | source)
XLA Modules:
  0.0 407.3 jit_solution(7129477333178125525)
XLA Ops:
  0.6 0.0 copy-start
  0.6 0.9 fusion.11
  1.5 0.2 reduce_window_sum.11
  1.7 0.8 select_reduce_fusion
  2.5 0.7 fusion.15
  3.2 1.4 convolution_convert_fusion
  4.6 0.1 copy.10
  4.7 13.1 %all_to_all.10 = bf16[2,4,24,2048]{3,2,0,1:T(8,128)(2,1)S(1)} all-to-all(bf16[2,4,24,2048]{3,2,0,1:T(8,128)(2,1)S(1)} %copy.10), channel_id=1, replica_groups=mesh['expert'=4,'fsdp'=32] {'expert'}, dimensions={1} | all-to-all | bytes 1572864 | tf_op jit(solution)/shard_map/all_to_all | solution.py:50
  17.8 0.1 copy.11
  17.8 3.2 stack.2
  21.0 297.8 %all_to_all.11 = bf16[32,2,4,24,2048]{4,3,2,1,0:T(8,128)(2,1)} all-to-all(bf16[32,2,4,24,2048]{4,3,2,1,0:T(8,128)(2,1)S(1)} %stack.2), channel_id=1, replica_groups=mesh['expert'=4,'fsdp'=32] {'fsdp'}, dimensions={0} | all-to-all | bytes 50331648 | tf_op jit(solution)/shard_map/all_to_all | solution.py:56
  318.8 0.0 copy-start.2
  318.8 21.2 %copy.12 = bf16[2,4,32,24,2048]{4,3,2,1,0:T(8,128)(2,1)} copy(bf16[2,4,32,24,2048]{4,3,1,0,2:T(8,128)(2,1)} %bitcast.12) | data formatting | bytes 50331648 | tf_op jit(solution)/shard_map/reshape | solution.py:55
  340.0 0.0 copy-done.2
  340.0 0.0 copy-start.1
  340.1 14.5 %fusion.18 = f32[2,3072,256]{2,1,0:T(8,128)} fusion(bf16[2,3072,2048]{2,1,0:T(8,128)(2,1)} %bitcast.13, bf16[2,2048,256]{2,1,0:T(8,128)(2,1)S(1)} %copy-done.2), kind=kOutput, calls=%fused_computation.28 | convolution fusion | flops 6442450944 | bytes 33554432 | tf_op jit(solution)/shard_map/grd,gdf->grf/dot_general | solution.py:12
  354.6 0.0 copy-done.1
  354.6 17.5 %fusion.5 = f32[2,2048,256]{2,1,0:T(8,128)} fusion(bf16[2,3072,2048]{2,1,0:T(8,128)(2,1)} %bitcast.14, bf16[2,3072,256]{2,1,0:T(8,128)(2,1)S(1)} %copy-done.1, f32[2,3072,256]{2,1,0:T(8,128)} %fusion.18), kind=kOutput, calls=%fused_computation.9 | convolution fusion | flops 6453460992 | bytes 38797312 | tf_op jit(solution)/shard_map/grd,grf->gdf/dot_general | solution.py:23
  372.0 0.0 copy-done
  372.0 16.1 %multiply_convert_fusion = (bf16[2,3072,256]{2,1,0:T(8,128)(2,1)}, f32[2,3072,256]{2,1,0:T(8,128)}) fusion(f32[2,3072,256]{2,1,0:T(8,128)} %fusion.18, bf16[2,3072,2048]{2,1,0:T(8,128)(2,1)} %bitcast.15, bf16[2,2048,256]{2,1,0:T(8,128)(2,1)S(1)} %copy-done), kind=kOutput, calls=%fused_computation.6 | convolution fusion | flops 6451888128 | bytes 42991616 | tf_op jit(solution)/shard_map/grd,gdf->grf/dot_general | solution.py:13
  388.1 19.2 %fusion.7 = f32[2,2048,256]{2,1,0:T(8,128)} fusion(bf16[2,3072,2048]{2,1,0:T(8,128)(2,1)} %bitcast.16, f32[2,3072,256]{2,1,0:T(8,128)} %get-tuple-element.4, bf16[2,3072,256]{2,1,0:T(8,128)(2,1)S(1)} %copy-done.1, f32[2,3072,256]{2,1,0:T(8,128)} %fusion.18), kind=kOutput, calls=%fused_computation.10 | convolution fusion | flops 6459752448 | bytes 45088768 | tf_op jit(solution)/shard_map/grd,grf->gdf/dot_general | solution.py:22
Async XLA Ops:
  0.6 371.4 %copy-start = (bf16[2,2048,256]{2,1,0:T(8,128)(2,1)S(1)}, bf16[2,2048,256]{2,1,0:T(8,128)(2,1)}, u32[]{:S(2)}) copy-start(bf16[2,2048,256]{2,1,0:T(8,128)(2,1)} %param.8) | copy-start | bytes 6291460
  318.8 21.2 %copy-start.2 = (bf16[2,2048,256]{2,1,0:T(8,128)(2,1)S(1)}, bf16[2,2048,256]{2,1,0:T(8,128)(2,1)}, u32[]{:S(2)}) copy-start(bf16[2,2048,256]{2,1,0:T(8,128)(2,1)} %param.7) | copy-start | bytes 6291460
  340.0 14.5 %copy-start.1 = (bf16[2,3072,256]{2,1,0:T(8,128)(2,1)S(1)}, bf16[2,3072,256]{2,1,0:T(8,128)(2,1)}, u32[]{:S(2)}) copy-start(bf16[2,3072,256]{2,1,0:T(8,128)(2,1)} %param.9) | copy-start | bytes 9437188
